TPU v7x, 32 devices: a whole 2x2x4 slice. The times are simulated.
32 devices in a mesh: fsdp: 8 (over y, x, core), dp: 4 (over z).
Axes of the slice: x: 2, y: 2, z: 4, core: 2. Of those that a mesh axis runs over, the one named last changes fastest.
Arguments:
- tokens: bfloat16 [131072, 1024], P(('fsdp', 'dp')), may hold values from -6 to 6
- cotangent: bfloat16 [131072, 1024], P(('fsdp', 'dp')), may hold values from -6 to 6
- lengths: int32 [256], P(('fsdp', 'dp')), may hold values from 8 to 2048, as said below
- selected: int32 [16384], P(('fsdp', 'dp')), may hold values from 0 to 4095, as said below
- attn_in: bfloat16 [1024, 3072], P('fsdp'), may hold values from -0.1875 to 0.1875
- attn_out: bfloat16 [1024, 1024], P('fsdp'), may hold values from -0.75 to 0.75
- mlp_in: bfloat16 [1024, 4096], P('fsdp'), may hold values from -0.1875 to 0.1875
- mlp_out: bfloat16 [4096, 1024], P('fsdp'), may hold values from -0.09375 to 0.09375
- norm_attn: bfloat16 [1024], P('fsdp'), may hold values from 0.5 to 1.5
- norm_mlp: bfloat16 [1024], P('fsdp'), may hold values from 0.5 to 1.5
- router: bfloat16 [1024], replicated, may hold values from -0.1875 to 0.1875
Outputs:
- output: bfloat16 [131072, 1024], P(('fsdp', 'dp'))
- grad_tokens: bfloat16 [131072, 1024], P(('fsdp', 'dp'))
- grad_attn_in: float32 [1024, 3072], P('fsdp')
- grad_attn_out: float32 [1024, 1024], P('fsdp')
- grad_mlp_in: float32 [1024, 4096], P('fsdp')
- grad_mlp_out: float32 [4096, 1024], P('fsdp')
- grad_norm_attn: float32 [1024], P('fsdp')
- grad_norm_mlp: float32 [1024], P('fsdp')
- grad_router: float32 [1024], replicated
Inputs may be any that keep to these rules, and one draw needn't show every extreme that they name: `lengths`: each aligned block of 8 entries (one device's sequences, in order) holds multiples of 8 that sum to 4096; exactly one of them equals 2048. `selected`: each aligned block of 512 entries lists distinct positions within its device's 4096 tokens in ascending order; a sequence of length L has exactly L / 8 of its positions listed.
All inputs are finite; a program needn't handle non-finite values.
Results may differ from a plain program's by a relative error of at most 0.014.
Values may be sent and summed in bfloat16 or wider, within the bound.
No kernel may reach another device: no remote copies, remote signals or barrier semaphores. Data moves between devices by JAX's collectives and lax.ppermute only.
A program may use at most 192 MiB of HBM per device.

v0:
```python
import jax
import jax.numpy as jnp
from jax import lax
from jax.sharding import PartitionSpec as P

HEADS = 16
HEAD = 64
EPS = 1e-06
MASKED = -1e30


def rms_scale(values, gain_vec):
    return values * lax.rsqrt(jnp.mean(values * values, axis=-1, keepdims=True) + EPS) * gain_vec


def seq_mask(lengths, selected):
    seq_ends = jnp.cumsum(lengths)
    owner_seq = jnp.sum((selected[:, None] >= seq_ends[None, :]).astype(jnp.int32), axis=1)
    return (owner_seq[:, None] == owner_seq[None, :]) & (selected[None, :] <= selected[:, None])


def split_heads(matrix):
    return matrix.reshape(matrix.shape[0], HEADS, HEAD)


def masked_scores(query_heads, key_heads, allowed, score_scale):
    scores = (
        jnp.einsum("qhd,khd->hqk", query_heads, key_heads, preferred_element_type=jnp.float32)
        * score_scale
    )
    return jnp.where(allowed[None], scores, MASKED)


def per_device(
    tokens,
    cotangent,
    lengths,
    selected,
    attn_in,
    attn_out,
    mlp_in,
    mlp_out,
    norm_attn,
    norm_mlp,
    router,
):
    model_width = tokens.shape[1]
    row_count = selected.shape[0]
    score_scale = HEAD ** (-0.5)
    w_qkv, w_out, gain_attn, gain_mlp = (
        lax.all_gather(attn_in, "fsdp", axis=0, tiled=True),
        lax.all_gather(attn_out, "fsdp", axis=0, tiled=True),
        lax.all_gather(norm_attn, "fsdp", axis=0, tiled=True),
        lax.all_gather(norm_mlp, "fsdp", axis=0, tiled=True),
    )
    w_in, w_down = (
        lax.all_gather(mlp_in, "fsdp", axis=0, tiled=True),
        lax.all_gather(mlp_out, "fsdp", axis=0, tiled=True),
    )
    gain_one = gain_attn.astype(jnp.float32)
    gain_two = gain_mlp.astype(jnp.float32)
    positions = lax.broadcasted_iota(jnp.int32, (row_count, tokens.shape[0]), 1)
    select = (selected[:, None] == positions).astype(jnp.bfloat16)
    routed = jnp.dot(select, tokens, preferred_element_type=jnp.float32)
    routed_low = routed.astype(jnp.bfloat16)
    router_rate = jnp.dot(routed_low, router, preferred_element_type=jnp.float32)
    allowed = seq_mask(lengths, selected)
    normed_float, norm_pull = jax.vjp(rms_scale, routed, gain_one)
    normed = normed_float.astype(jnp.bfloat16)
    qkv = jnp.dot(normed, w_qkv, preferred_element_type=jnp.float32).astype(jnp.bfloat16)
    query_heads = split_heads(qkv[:, :model_width])
    key_heads = split_heads(qkv[:, model_width : 2 * model_width])
    value_heads = split_heads(qkv[:, 2 * model_width :])
    scores = masked_scores(query_heads, key_heads, allowed, score_scale)
    highest = jnp.max(scores, axis=-1, keepdims=True)
    exponent = jnp.exp(scores - highest)
    row_total = jnp.sum(exponent, axis=-1, keepdims=True)
    probabilities = (exponent / row_total).astype(jnp.bfloat16)
    log_total = highest + jnp.log(row_total)
    attn_mix = jnp.einsum(
        "hqk,khd->qhd", probabilities, value_heads, preferred_element_type=jnp.float32
    )
    attn_mix = attn_mix.reshape(row_count, model_width).astype(jnp.bfloat16)
    attended = jnp.dot(attn_mix, w_out, preferred_element_type=jnp.float32)
    middle = routed + attended
    normed_two_float, middle_pull = jax.vjp(rms_scale, middle, gain_two)
    normed_two = normed_two_float.astype(jnp.bfloat16)
    pre_gelu = jnp.dot(normed_two, w_in, preferred_element_type=jnp.float32)
    active_float, gelu_pull = jax.vjp(jax.nn.gelu, pre_gelu)
    active = active_float.astype(jnp.bfloat16)
    expanded = jnp.dot(active, w_down, preferred_element_type=jnp.float32)
    update = attended + expanded
    branch = (router_rate[:, None] * update).astype(jnp.bfloat16)
    output = (
        tokens.astype(jnp.float32)
        + jnp.einsum("kt,kd->td", select, branch, preferred_element_type=jnp.float32)
    ).astype(jnp.bfloat16)
    w_qkv_back, w_out_back = (
        lax.all_gather(attn_in, "fsdp", axis=0, tiled=True),
        lax.all_gather(attn_out, "fsdp", axis=0, tiled=True),
    )
    w_in_back, w_down_back = (
        lax.all_gather(mlp_in, "fsdp", axis=0, tiled=True),
        lax.all_gather(mlp_out, "fsdp", axis=0, tiled=True),
    )
    cot_rows = jnp.dot(select, cotangent, preferred_element_type=jnp.float32)
    grad_rate = jnp.sum(cot_rows * update, axis=-1)
    grad_update = cot_rows * router_rate[:, None]
    grad_expanded = grad_update.astype(jnp.bfloat16)
    grad_down = jnp.einsum("kf,kd->fd", active, grad_expanded, preferred_element_type=jnp.float32)
    grad_active = jnp.einsum(
        "kd,fd->kf", grad_expanded, w_down_back, preferred_element_type=jnp.float32
    )
    (grad_inner_float,) = gelu_pull(grad_active)
    grad_inner = grad_inner_float.astype(jnp.bfloat16)
    grad_up = jnp.einsum("kd,kf->df", normed_two, grad_inner, preferred_element_type=jnp.float32)
    grad_normed_two = jnp.einsum(
        "kf,df->kd", grad_inner, w_in_back, preferred_element_type=jnp.float32
    )
    grad_middle, grad_gain_two = middle_pull(grad_normed_two)
    grad_attended = (grad_update + grad_middle).astype(jnp.bfloat16)
    grad_proj = jnp.einsum("ka,kd->ad", attn_mix, grad_attended, preferred_element_type=jnp.float32)
    grad_mix = jnp.einsum(
        "kd,ad->ka", grad_attended, w_out_back, preferred_element_type=jnp.float32
    ).astype(jnp.bfloat16)
    grad_mix_heads = split_heads(grad_mix)
    scores_again = masked_scores(query_heads, key_heads, allowed, score_scale)
    prob_float = jnp.where(allowed[None], jnp.exp(scores_again - log_total), 0.0)
    grad_probs = jnp.einsum(
        "qhd,khd->hqk", grad_mix_heads, value_heads, preferred_element_type=jnp.float32
    )
    row_delta = jnp.sum(prob_float * grad_probs, axis=-1, keepdims=True)
    grad_scores = (prob_float * (grad_probs - row_delta)).astype(jnp.bfloat16)
    prob_low = prob_float.astype(jnp.bfloat16)
    grad_query = (
        jnp.einsum("hqk,khd->qhd", grad_scores, key_heads, preferred_element_type=jnp.float32)
        * score_scale
    )
    grad_key = (
        jnp.einsum("hqk,qhd->khd", grad_scores, query_heads, preferred_element_type=jnp.float32)
        * score_scale
    )
    grad_value = jnp.einsum(
        "hqk,qhd->khd", prob_low, grad_mix_heads, preferred_element_type=jnp.float32
    )
    grad_qkv = jnp.concatenate(
        [
            grad_query.reshape(row_count, model_width),
            grad_key.reshape(row_count, model_width),
            grad_value.reshape(row_count, model_width),
        ],
        axis=1,
    ).astype(jnp.bfloat16)
    grad_proj_in = jnp.einsum("kd,ke->de", normed, grad_qkv, preferred_element_type=jnp.float32)
    grad_normed = jnp.einsum("ke,de->kd", grad_qkv, w_qkv_back, preferred_element_type=jnp.float32)
    grad_routed_norm, grad_gain_one = norm_pull(grad_normed)
    grad_routed = (
        grad_routed_norm + grad_middle + grad_rate[:, None] * router.astype(jnp.float32)
    ).astype(jnp.bfloat16)
    grad_tokens = (
        cotangent.astype(jnp.float32)
        + jnp.einsum("kt,kd->td", select, grad_routed, preferred_element_type=jnp.float32)
    ).astype(jnp.bfloat16)
    router_local = jnp.dot(grad_rate, routed, precision=lax.Precision.HIGHEST)
    shard_up, shard_down, shard_gain_two = (
        lax.psum_scatter(grad_up, "fsdp", scatter_dimension=0, tiled=True),
        lax.psum_scatter(grad_down, "fsdp", scatter_dimension=0, tiled=True),
        lax.psum_scatter(grad_gain_two, "fsdp", scatter_dimension=0, tiled=True),
    )
    shard_qkv, shard_proj, shard_gain_one = (
        lax.psum_scatter(grad_proj_in, "fsdp", scatter_dimension=0, tiled=True),
        lax.psum_scatter(grad_proj, "fsdp", scatter_dimension=0, tiled=True),
        lax.psum_scatter(grad_gain_one, "fsdp", scatter_dimension=0, tiled=True),
    )
    summed = (
        lax.psum(shard_qkv.astype(jnp.bfloat16), "dp").astype(jnp.float32),
        lax.psum(shard_proj.astype(jnp.bfloat16), "dp").astype(jnp.float32),
        lax.psum(shard_up.astype(jnp.bfloat16), "dp").astype(jnp.float32),
        lax.psum(shard_down.astype(jnp.bfloat16), "dp").astype(jnp.float32),
        lax.psum(shard_gain_one.astype(jnp.bfloat16), "dp").astype(jnp.float32),
        lax.psum(shard_gain_two.astype(jnp.bfloat16), "dp").astype(jnp.float32),
    )
    grad_router = lax.psum(router_local, ("fsdp", "dp"))
    return (
        output,
        grad_tokens,
        summed[0],
        summed[1],
        summed[2],
        summed[3],
        summed[4],
        summed[5],
        grad_router,
    )


def solution(mesh):
    placed = (
        P(("fsdp", "dp"), None),
        P(("fsdp", "dp"), None),
        P(("fsdp", "dp")),
        P(("fsdp", "dp")),
        P("fsdp", None),
        P("fsdp", None),
        P("fsdp", None),
        P("fsdp", None),
        P("fsdp"),
        P("fsdp"),
        P(),
    )
    return jax.shard_map(
        per_device,
        mesh=mesh,
        in_specs=placed,
        out_specs=(
            P(("fsdp", "dp"), None),
            P(("fsdp", "dp"), None),
            P("fsdp", None),
            P("fsdp", None),
            P("fsdp", None),
            P("fsdp", None),
            P("fsdp"),
            P("fsdp"),
            P(),
        ),
        check_vma=False,
    )
```

profile of v0, /device:TPU:0, one launch (start us, length us, event | category | flops | bytes accessed | tf_op | source)
XLA Modules:
  0.0 773.5 jit_solution(13917479941379814595)
XLA Ops:
  10.0 10.4 %all-gather = bf16[8,1,128]{2,1,0:T(2,128)(2,1)S(1)} all-gather(bf16[1,1,128]{2,1,0:T(2,128)(2,1)} %bitcast.84), channel_id=1, replica_groups=mesh['fsdp'=8,'dp'=4] {'fsdp'}, dimensions={0}, use_global_device_ids=true | all-gather | bytes 2304 | tf_op jit(solution)/shard_map/all_gather | solution.py:53
  20.4 8.9 %all-gather.1 = bf16[8,1,128]{2,1,0:T(2,128)(2,1)S(1)} all-gather(bf16[1,1,128]{2,1,0:T(2,128)(2,1)} %bitcast.85), channel_id=1, replica_groups=mesh['fsdp'=8,'dp'=4] {'fsdp'}, dimensions={0}, use_global_device_ids=true | all-gather | bytes 2304 | tf_op jit(solution)/shard_map/all_gather | solution.py:54
  31.6 7.8 %multiply_reduce_fusion.7 = (f32[512]{0:T(512)S(1)}, f32[512,1024]{1,0:T(8,128)S(1)}) fusion(bf16[4096,1024]{1,0:T(8,128)(2,1)} %param.11, s32[512]{0:T(512)} %param.14), kind=kOutput, calls=%fused_computation.51 | convolution fusion | flops 4298112512 | bytes 10489856 | tf_op jit(solution)/shard_map/dot_general | solution.py:64
  40.1 9.3 %fusion.12 = f32[512,1024]{1,0:T(8,128)} fusion(bf16[4096,1024]{1,0:T(8,128)(2,1)} %param.12, s32[512]{0:T(512)S(1)} %copy-done.10), kind=kOutput, calls=%fused_computation.24 | convolution fusion | flops 4297064448 | bytes 10487808 | tf_op jit(solution)/shard_map/dot_general | solution.py:106
  49.4 8.7 %all-gather.7.cloned.1.call-done = bf16[1024,3072]{1,0:T(8,128)(2,1)} async-done(((bf16[128,3072]{1,0:T(8,128)(2,1)}), bf16[1024,3072]{1,0:T(8,128)(2,1)}) %all-gather.7.cloned.1.call-update) | async-done | bytes 6291472 | tf_op jit(solution)/shard_map/all_gather | solution.py:51
  58.0 6.6 convolution_convert_fusion
  64.6 1.7 fusion.51
  66.4 1.5 copy.50
  67.9 2.3 copy.49
  70.2 2.3 copy.48
  72.4 9.1 %fusion.1 = (f32[16,512]{1,0:T(8,128)S(1)}, f32[16,512,512]{1,2,0:T(8,128)}) fusion(pred[512,512]{0,1:T(8,128)(4,1)S(1)} %compare_and_fusion, bf16[512,16,64]{0,2,1:T(8,128)(2,1)} %bitcast.57, bf16[512,16,64]{0,2,1:T(8,128)(2,1)S(1)} %bitcast.55), kind=kOutput, calls=%fused_computation.11 | convolution fusion | flops 549445632 | bytes 19169280 | tf_op jit(solution)/shard_map/qhd,khd->hqk/dot_general | solution.py:28
  81.5 9.3 %fusion = f32[16,512]{1,0:T(8,128)S(1)} fusion(f32[16,512,512]{1,2,0:T(8,128)} %get-tuple-element.31, f32[16,512]{1,0:T(8,128)S(1)} %get-tuple-element.30, pred[512,512]{0,1:T(8,128)(4,1)S(1)} %compare_and_fusion), kind=kLoop, calls=%fused_computation.8 | loop fusion | flops 16769024 | bytes 17104896 | tf_op jit(solution)/shard_map/reduce_sum | solution.py:77
  90.8 9.6 %fusion.23 = bf16[16,64,512]{2,1,0:T(8,128)(2,1)} fusion(bf16[512,16,64]{0,2,1:T(8,128)(2,1)} %bitcast.65, f32[16,512,512]{1,2,0:T(8,128)} %get-tuple-element.31, f32[16,512]{1,0:T(8,128)S(1)} %fusion, f32[16,512]{1,0:T(8,128)S(1)} %get-tuple-element.30, pred[512,512]{0,1:T(8,128)(4,1)S(1)} %compare_and_fusion), kind=kOutput, calls=%fused_computation.54 | convolution fusion | flops 558366720 | bytes 19202048 | tf_op jit(solution)/shard_map/hqk,khd->qhd/dot_general | solution.py:80
  100.4 5.2 multiply_reduce_fusion.6
  105.6 38.3 %all-gather.11.cloned.1.call-done = bf16[1024,4096]{1,0:T(8,128)(2,1)} async-done(((bf16[128,4096]{1,0:T(8,128)(2,1)}), bf16[1024,4096]{1,0:T(8,128)(2,1)}) %all-gather.11.cloned.1.call-update) | async-done | bytes 8388624 | tf_op jit(solution)/shard_map/all_gather | solution.py:57
  143.9 12.1 %fusion.50 = f32[512,4096]{1,0:T(8,128)} fusion(bf16[1024,4096]{1,0:T(8,128)(2,1)} %all-gather.11.cloned.1.call-done, f32[512,1024]{1,0:T(8,128)} %get-tuple-element.22, f32[1024]{0:T(1024)S(1)} %bitcast.74, f32[512]{0:T(512)S(1)} %fusion.39), kind=kOutput, calls=%fused_computation.88 | convolution fusion | flops 4296540160 | bytes 18880512 | tf_op jit(solution)/shard_map/dot_general | solution.py:88
  156.0 44.0 %all-gather.13.cloned.1.call-done = bf16[4096,1024]{1,0:T(8,128)(2,1)} async-done(((bf16[512,1024]{1,0:T(8,128)(2,1)}), bf16[4096,1024]{1,0:T(8,128)(2,1)}) %all-gather.13.cloned.1.call-update) | async-done | bytes 8388624 | tf_op jit(solution)/shard_map/all_gather | solution.py:58
  200.0 14.6 %fusion.8 = bf16[512,4096]{1,0:T(8,128)(2,1)} fusion(f32[512,4096]{1,0:T(8,128)} %fusion.50, bf16[4096,1024]{1,0:T(8,128)(2,1)} %all-gather.13.cloned.1.call-done, f32[512,1024]{1,0:T(8,128)} %fusion.12, f32[512]{0:T(512)S(1)} %bitcast.79), kind=kOutput, calls=%fused_computation.18 | convolution fusion | flops 4337958912 | bytes 23070720 | tf_op jit(solution)/shard_map/kd,fd->kf/dot_general | solution.py:111
  214.6 10.9 %multiply_reduce_fusion.1 = (f32[1024]{0:T(1024)S(1)}, f32[512]{0:T(512)S(1)}, f32[512,1024]{1,0:T(8,128)}) fusion(f32[512,1024]{1,0:T(8,128)S(1)} %copy-done.1, f32[512]{0:T(512)S(1)} %fusion.39, f32[1024]{0:T(1024)S(1)} %bitcast.75, bf16[512,4096]{1,0:T(8,128)(2,1)} %fusion.8, bf16[1024,4096]{1,0:T(8,128)(2,1)} %all-gather.11.cloned.1.call-done), kind=kOutput, calls=%fused_computation.39 | convolution fusion | flops 4298111488 | bytes 16789504 | tf_op jit(solution)/shard_map/kf,df->kd/dot_general | solution.py:117
  225.5 10.1 %multiply_reduce_fusion.3 = (f32[512]{0:T(512)S(1)}, bf16[512,1024]{1,0:T(8,128)(2,1)S(1)}, f32[512,1024]{1,0:T(8,128)}) fusion(f32[512,1024]{1,0:T(8,128)S(1)} %copy-done.19, f32[512,1024]{1,0:T(8,128)S(1)} %copy-done.1, f32[512]{0:T(512)S(1)} %multiply_multiply_fusion.3, f32[512]{0:T(512)S(1)} %fusion.39, f32[512,1024]{1,0:T(8,128)} %get-tuple-element.33, ...), kind=kOutput, calls=%fused_computation.41 | convolution fusion | flops 4319608320 | bytes 28323840 | tf_op jit(solution)/shard_map/dot_general | solution.py:91
  236.6 3.2 fusion.52
  239.8 4.2 convolution_convert_fusion.1
  244.0 2.3 copy.52
  246.4 13.6 %multiply_reduce_fusion = (f32[16,512]{1,0:T(8,128)S(1)}, f32[16,512,512]{1,2,0:T(8,128)}) fusion(f32[16,512]{1,0:T(8,128)S(1)} %log_add_fusion, f32[16,512,512]{1,2,0:T(8,128)} %get-tuple-element.31, pred[512,512]{0,1:T(8,128)(4,1)S(1)} %compare_and_fusion, bf16[512,16,64]{0,2,1:T(8,128)(2,1)} %bitcast.67, bf16[512,16,64]{0,2,1:T(8,128)(2,1)} %bitcast.66), kind=kOutput, calls=%fused_computation.2 | convolution fusion | flops 562028544 | bytes 35979264 | tf_op jit(solution)/shard_map/qhd,khd->hqk/dot_general | solution.py:129
  259.9 13.2 %multiply_convert_fusion = bf16[16,512,512]{1,2,0:T(8,128)(2,1)S(1)} fusion(f32[16,512,512]{1,2,0:T(8,128)} %get-tuple-element.36, f32[16,512]{1,0:T(8,128)S(1)} %get-tuple-element.35, f32[16,512]{1,0:T(8,128)S(1)} %log_add_fusion, f32[16,512,512]{1,2,0:T(8,128)} %get-tuple-element.31, pred[512,512]{0,1:T(8,128)(4,1)S(1)} %compare_and_fusion), kind=kLoop, calls=%fused_computation.1 | loop fusion | flops 29360128 | bytes 42270720 | tf_op jit(solution)/shard_map/convert_element_type | solution.py:133
  273.1 2.6 multiply_convert_fusion.2
  275.8 1.5 multiply_convert_fusion.3
  277.4 8.6 %fusion.24 = bf16[16,64,512]{2,1,0:T(8,128)(2,1)S(1)} fusion(bf16[512,16,64]{0,2,1:T(8,128)(2,1)S(1)} %bitcast.68, f32[16,512]{1,0:T(8,128)S(1)} %log_add_fusion, f32[16,512,512]{1,2,0:T(8,128)} %get-tuple-element.31, pred[512,512]{0,1:T(8,128)(4,1)S(1)} %compare_and_fusion), kind=kOutput, calls=%fused_computation.56 | convolution fusion | flops 558366720 | bytes 19169280 | tf_op jit(solution)/shard_map/hqk,qhd->khd/dot_general | solution.py:143
  287.0 9.9 %fusion.27 = f32[1024,3072]{1,0:T(8,128)} fusion(bf16[512,1024]{0,1:T(8,128)(2,1)S(1)} %bitcast.88, bf16[512,1024]{0,1:T(8,128)(2,1)S(1)} %bitcast.63, bf16[512,1024]{0,1:T(8,128)(2,1)S(1)} %bitcast.59, f32[512,1024]{1,0:T(8,128)S(1)} %get-tuple-element.29, f32[1024]{0:T(1024)S(1)} %bitcast.71, f32[512]{0:T(512)S(1)} %fusion.38), kind=kOutput, calls=%fused_computation.57 | convolution fusion | flops 3232235520 | bytes 17831936 | tf_op jit(solution)/shard_map/kd,ke->de/dot_general | solution.py:154
  296.9 19.0 %fusion.47 = f32[4096,1024]{1,0:T(8,128)} fusion(f32[512,1024]{1,0:T(8,128)} %fusion.12, f32[512]{0:T(512)S(1)} %bitcast.81, f32[512,4096]{1,0:T(8,128)} %fusion.50), kind=kOutput, calls=%fused_computation.85 | convolution fusion | flops 4314890240 | bytes 27265024 | tf_op jit(solution)/shard_map/kf,kd->fd/dot_general | solution.py:110
  316.2 15.3 %fusion.49 = f32[1024,4096]{1,0:T(8,128)} fusion(bf16[512,4096]{1,0:T(8,128)(2,1)} %fusion.8, f32[512,1024]{1,0:T(8,128)} %get-tuple-element.22, f32[1024]{0:T(1024)S(1)} %bitcast.77, f32[512]{0:T(512)S(1)} %fusion.39), kind=kOutput, calls=%fused_computation.87 | convolution fusion | flops 4296540160 | bytes 23074816 | tf_op jit(solution)/shard_map/kd,kf->df/dot_general | solution.py:116
  333.5 8.4 %multiply_reduce_fusion.2 = (f32[1024]{0:T(1024)S(1)}, f32[512]{0:T(512)S(1)}, f32[512,1024]{1,0:T(8,128)}) fusion(f32[512,1024]{1,0:T(8,128)S(1)} %get-tuple-element.29, f32[512]{0:T(512)S(1)} %fusion.38, f32[1024]{0:T(1024)S(1)} %bitcast.72, bf16[1024,3072]{1,0:T(8,128)(2,1)} %all-gather.7.cloned.1.call-done, bf16[512,1024]{0,1:T(8,128)(2,1)} %bitcast.89, ...), kind=kOutput, calls=%fused_computation.40 | convolution fusion | flops 3233806848 | bytes 13643776 | tf_op jit(solution)/shard_map/ke,de->kd/dot_general | solution.py:155
  341.9 15.5 %all-reduce.2 = (bf16[1024]{0:T(1024)(128)(2,1)S(1)}, bf16[1024]{0:T(1024)(128)(2,1)S(1)}) all-reduce(f32[1024]{0:T(1024)S(1)} %get-tuple-element.11, f32[1024]{0:T(1024)S(1)} %get-tuple-element.9), channel_id=6, replica_groups=mesh['fsdp'=8,'dp'=4] {'fsdp'}, use_global_device_ids=true, to_apply=%region_19.20.clone | all-reduce | flops 2048 | bytes 12288
  357.6 11.7 %all-reduce.3 = (bf16[128]{0:T(256)(128)(2,1)S(1)}, bf16[128]{0:T(256)(128)(2,1)S(1)}) all-reduce(bf16[128]{0:T(256)(128)(2,1)S(1)} %dynamic-slice.7, bf16[128]{0:T(256)(128)(2,1)S(1)} %dynamic-slice.6), channel_id=1, replica_groups=mesh['fsdp'=8,'dp'=4] {'dp'}, use_global_device_ids=true, to_apply=%region_20.21 | all-reduce | flops 256 | bytes 1024 | tf_op jit(solution)/shard_map/psum | solution.py:180
  371.4 37.7 %psum.55 = f32[1024]{0:T(1024)} all-reduce(f32[1024]{0:T(1024)S(1)} %bitcast.69), channel_id=1, replica_groups=mesh['fsdp'=8,'dp'=4] {'fsdp','dp'}, use_global_device_ids=true, to_apply=%region_24.25 | all-reduce | flops 1024 | bytes 8192 | tf_op jit(solution)/shard_map/psum | solution.py:183
  409.2 1.8 convert_element_type.140
  411.1 2.6 convert_element_type.138
  413.7 100.4 %reduce-scatter.11.cloned.1.call-done = f32[512,1024]{1,0:T(8,128)} async-done(((f32[4096,1024]{1,0:T(8,128)}), f32[512,1024]{1,0:T(8,128)}) %reduce-scatter.11.cloned.1.call-update) | async-done | bytes 2097168 | tf_op jit(solution)/shard_map/reduce_scatter | solution.py:167
  514.0 2.7 convert_element_type.144
  516.8 117.0 %reduce-scatter.9.cloned.1.call-done = f32[128,4096]{1,0:T(8,128)} async-done(((f32[1024,4096]{1,0:T(8,128)}), f32[128,4096]{1,0:T(8,128)}) %reduce-scatter.9.cloned.1.call-update) | async-done | bytes 2097168 | tf_op jit(solution)/shard_map/reduce_scatter | solution.py:166
  633.8 2.7 convert_element_type.142
  636.6 10.0 %add_convert_fusion.1 = bf16[4096,1024]{1,0:T(8,128)(2,1)} fusion(bf16[4096,1024]{1,0:T(8,128)(2,1)} %param.11, s32[512]{0:T(512)S(1)} %copy-done.11, f32[512,1024]{1,0:T(8,128)} %get-tuple-element.34, f32[512]{0:T(512)S(1)} %bitcast.82), kind=kOutput, calls=%fused_computation.4 | convolution fusion | flops 4310695936 | bytes 18878464 | tf_op jit(solution)/shard_map/kt,kd->td/dot_general | solution.py:96
  646.6 11.4 %add_convert_fusion = bf16[4096,1024]{1,0:T(8,128)(2,1)} fusion(bf16[4096,1024]{1,0:T(8,128)(2,1)} %param.12, s32[512]{0:T(512)S(1)} %copy-done.11, f32[512,1024]{1,0:T(8,128)S(1)} %get-tuple-element.29, f32[512,1024]{1,0:T(8,128)S(1)} %copy-done.20, f32[1024]{0:T(1024)S(1)} %convert_element_type.135, f32[512]{0:T(512)S(1)} %get-tuple-element.26, ...), kind=kOutput, calls=%fused_computation | convolution fusion | flops 4316987392 | bytes 25190400 | tf_op jit(solution)/shard_map/kt,kd->td/dot_general | solution.py:162
  658.0 100.1 %all-reduce.7.cloned.1.call-done = (bf16[128,3072]{1,0:T(8,128)(2,1)}, bf16[128,1024]{1,0:T(8,128)(2,1)}, bf16[128,4096]{1,0:T(8,128)(2,1)}, bf16[512,1024]{1,0:T(8,128)(2,1)}) async-done(((bf16[128,3072]{1,0:T(8,128)(2,1)}, bf16[128,1024]{1,0:T(8,128)(2,1)}, bf16[128,4096]{1,0:T(8,128)(2,1)}, bf16[512,1024]{1,0:T(8,128)(2,1)}), (bf16[128,3072]{1,0:T(8,128)(2,1)}, bf16[128,1024]{1,0:T(8,128)(2,1)}, ...) | async-done | bytes 3145744 | tf_op jit(solution)/shard_map/psum | solution.py:176
  758.1 1.9 convert_element_type.141
  760.0 2.4 convert_element_type.139
  762.5 2.8 convert_element_type.143
  765.2 1.6 convert_element_type.145
  (84 shorter events, 11.8 us)
Async XLA Ops:
  7.2 50.9 %all-gather.7.cloned.1.call-start = ((), (), s32[]{:S(2)}) async-start(), calls=%async_computation.4 | async-start | bytes 7077888 | tf_op jit(solution)/shard_map/all_gather | solution.py:51
  7.9 92.5 %all-gather.9.cloned.1.call-start = ((), (), s32[]{:S(2)}) async-start(), calls=%async_computation.5 | async-start | bytes 2359296 | tf_op jit(solution)/shard_map/all_gather | solution.py:52
  8.7 135.3 %all-gather.11.cloned.1.call-start = ((), (), s32[]{:S(2)}) async-start(), calls=%async_computation.6 | async-start | bytes 9437184 | tf_op jit(solution)/shard_map/all_gather | solution.py:57
  9.4 190.6 %all-gather.13.cloned.1.call-start = ((), (), s32[]{:S(2)}) async-start(), calls=%async_computation.7 | async-start | bytes 9437184 | tf_op jit(solution)/shard_map/all_gather | solution.py:58
  10.0 399.2 %reduce-scatter.7.cloned.1.call-start = ((), (), s32[]{:S(2)}) async-start(), calls=%async_computation.9 | async-start | bytes 4718592 | tf_op jit(solution)/shard_map/reduce_scatter | solution.py:172
  31.6 7.8 %copy-start.10 = (s32[512]{0:T(512)S(1)}, s32[512]{0:T(512)}, u32[]{:S(2)}) copy-start(s32[512]{0:T(512)} %param.14) | copy-start | bytes 6148
  39.4 0.7 copy-start.13
  200.0 14.6 %copy-start.1 = (f32[512,1024]{1,0:T(8,128)S(1)}, f32[512,1024]{1,0:T(8,128)}, u32[]{:S(2)}) copy-start(f32[512,1024]{1,0:T(8,128)} %get-tuple-element.22) | copy-start | bytes 6291460
  214.6 10.9 %copy-start.3 = (f32[512,1024]{1,0:T(8,128)S(1)}, f32[512,1024]{1,0:T(8,128)}, u32[]{:S(2)}) copy-start(f32[512,1024]{1,0:T(8,128)} %get-tuple-element.32) | copy-start | bytes 6291460
  214.6 10.9 %copy-start.15 = (bf16[4096,1024]{1,0:T(8,128)(2,1)S(1)}, bf16[4096,1024]{1,0:T(8,128)(2,1)}, u32[]{:S(2)}) copy-start(bf16[4096,1024]{1,0:T(8,128)(2,1)} %all-gather.13.cloned.1.call-done) | copy-start | bytes 25165828
  214.6 10.9 %copy-start.19 = (f32[512,1024]{1,0:T(8,128)S(1)}, f32[512,1024]{1,0:T(8,128)}, u32[]{:S(2)}) copy-start(f32[512,1024]{1,0:T(8,128)} %fusion.12) | copy-start | bytes 6291460
  225.5 11.1 %copy-start.6 = (bf16[16,64,512]{2,1,0:T(8,128)(2,1)S(1)}, bf16[16,64,512]{2,1,0:T(8,128)(2,1)}, u32[]{:S(2)}) copy-start(bf16[16,64,512]{2,1,0:T(8,128)(2,1)} %fusion.23) | copy-start | bytes 3145732
  235.6 1.0 copy-start.18
  246.3 164.7 %reduce-scatter.5.cloned.1.call-start = ((), (), s32[]{:S(2)}) async-start(), calls=%async_computation.8 | async-start | bytes 14155776 | tf_op jit(solution)/shard_map/reduce_scatter | solution.py:171
  259.9 13.2 %copy-start = (bf16[512,1024]{0,1:T(8,128)(2,1)S(1)}, bf16[512,1024]{0,1:T(8,128)(2,1)}, u32[]{:S(2)}) copy-start(bf16[512,1024]{0,1:T(8,128)(2,1)} %copy.49) | copy-start | bytes 3145732
  275.7 10.3 %copy-start.7 = (bf16[16,64,512]{2,1,0:T(8,128)(2,1)}, bf16[16,64,512]{2,1,0:T(8,128)(2,1)S(1)}, u32[]{:S(2)}) copy-start(bf16[16,64,512]{2,1,0:T(8,128)(2,1)S(1)} %multiply_convert_fusion.2) | copy-start | bytes 3145732
  275.8 1.6 copy-start.9
  277.4 8.7 %copy-start.4 = (bf16[16,64,512]{2,1,0:T(8,128)(2,1)}, bf16[16,64,512]{2,1,0:T(8,128)(2,1)S(1)}, u32[]{:S(2)}) copy-start(bf16[16,64,512]{2,1,0:T(8,128)(2,1)S(1)} %multiply_convert_fusion.3) | copy-start | bytes 3145732
  286.0 1.0 copy-start.16
  296.9 217.2 %reduce-scatter.11.cloned.1.call-start = ((), (), s32[]{:S(2)}) async-start(), calls=%async_computation.11 | async-start | bytes 18874368 | tf_op jit(solution)/shard_map/reduce_scatter | solution.py:167
  316.0 317.8 %reduce-scatter.9.cloned.1.call-start = ((), (), s32[]{:S(2)}) async-start(), calls=%async_computation.10 | async-start | bytes 18874368 | tf_op jit(solution)/shard_map/reduce_scatter | solution.py:166
  331.5 0.7 copy-start.12
  331.5 0.7 copy-start.17
  331.5 1.9 copy-start.5
  331.6 426.6 %all-reduce.7.cloned.1.call-start = ((), (), s32[]{:S(2)}) async-start(), calls=%async_computation.12 | async-start | bytes 6291456 | tf_op jit(solution)/shard_map/psum | solution.py:176
  333.5 75.7 %copy-start.14 = (f32[512]{0:T(512)S(1)}, f32[512]{0:T(512)}, u32[]{:S(2)}) copy-start(f32[512]{0:T(512)} %copy-done.13) | copy-start | bytes 6148
  409.2 227.4 %copy-start.11 = (s32[512]{0:T(512)S(1)}, s32[512]{0:T(512)}, u32[]{:S(2)}) copy-start(s32[512]{0:T(512)} %param.14) | copy-start | bytes 6148
  636.5 10.1 %copy-start.2 = (f32[512,1024]{1,0:T(8,128)S(1)}, f32[512,1024]{1,0:T(8,128)}, u32[]{:S(2)}) copy-start(f32[512,1024]{1,0:T(8,128)} %get-tuple-element.22) | copy-start | bytes 6291460
  636.6 10.1 %copy-start.20 = (f32[512,1024]{1,0:T(8,128)S(1)}, f32[512,1024]{1,0:T(8,128)}, u32[]{:S(2)}) copy-start(f32[512,1024]{1,0:T(8,128)} %get-tuple-element.37) | copy-start | bytes 6291460
  636.6 10.0 %copy-start.21 = (f32[512,1024]{1,0:T(8,128)S(1)}, f32[512,1024]{1,0:T(8,128)}, u32[]{:S(2)}) copy-start(f32[512,1024]{1,0:T(8,128)} %get-tuple-element.33) | copy-start | bytes 6291460
  758.1 7.1 copy-start.8
Sparse Core Ops, SparseCore 0:
  9.9 48.1 all-gather.6
  59.9 27.7 all-gather.8
  89.6 54.2 all-gather.10
  145.7 54.2 all-gather.12
  246.4 51.1 reduce-scatter.6
  301.0 93.5 reduce-scatter.4
  398.2 115.8 reduce-scatter.10
  517.6 116.1 reduce-scatter.8
  637.0 121.0 all-reduce.6
where the time goes:
time: 783 us; the launch traced here: 774 us
  waiting for transfers between devices  411 us (52%)
  matrix products  204 us (26%)
  blocking collectives  84.2 us (11%)
  other arithmetic  44 us (6%)
  between operations  15 us (2%)
  local copies, waits for them, and re-layouts  14.3 us (2%)
    reduce_scatter x1, waiting for transfers between devices, per_device(): lax.psum_scatter(grad_up, 'fsdp', scatter_dimension=0, tiled=True)  117 us
    reduce_scatter x1, waiting for transfers between devices, per_device(): lax.psum_scatter(grad_down, 'fsdp', scatter_dimension=0, tiled=True)  100 us
    psum x1, waiting for transfers between devices, per_device(): lax.psum(shard_qkv.astype(jnp.bfloat16), 'dp').astype(jnp.float32)  100 us
    all_gather x1, waiting for transfers between devices, per_device(): lax.all_gather(mlp_out, 'fsdp', axis=0, tiled=True)  44 us
    all_gather x1, waiting for transfers between devices, per_device(): lax.all_gather(mlp_in, 'fsdp', axis=0, tiled=True)  38.3 us
    psum x1, blocking collectives, per_device(): grad_router = lax.psum(router_local, ('fsdp', 'dp'))  37.7 us
    dot_general x1, matrix products, per_device(): jnp.einsum('kf,kd->fd', active, grad_expanded, preferred_element_type=jnp...  19 us
  transfers between devices with their start and end apart: 9, of which 6 were waited for; matrix products, arithmetic and copies ran while one was open for 26% of the time, Pallas kernels for 0%

commit v1 on v0

--- a/solution.py
+++ b/solution.py
@@ -7,6 +7,23 @@
 HEAD = 64
 EPS = 1e-06
 MASKED = -1e30
+
+
+def joined_along(parts, dim):
+    shape = list(parts.shape[1:])
+    shape[dim] *= parts.shape[0]
+    return jnp.moveaxis(parts, 0, dim).reshape(shape)
+
+
+def ring_gather(array, axis, dim):
+    size = lax.axis_size(axis)
+    right = [(i, (i + 1) % size) for i in range(size)]
+    blocks = [array]
+    while len(blocks) < size:
+        blocks.append(lax.ppermute(blocks[-1], axis, right))
+    index = lax.axis_index(axis)
+    blocks = jnp.stack(blocks)[(index - jnp.arange(size)) % size]
+    return joined_along(blocks, dim)
 
 
 def rms_scale(values, gain_vec):
@@ -54,7 +71,7 @@
         lax.all_gather(norm_mlp, "fsdp", axis=0, tiled=True),
     )
     w_in, w_down = (
-        lax.all_gather(mlp_in, "fsdp", axis=0, tiled=True),
+        ring_gather(mlp_in, "fsdp", 0),
         lax.all_gather(mlp_out, "fsdp", axis=0, tiled=True),
     )
     gain_one = gain_attn.astype(jnp.float32)

time: 783 us -> 839 us (1.072)
  waiting for transfers between devices: 411 us -> 443 us
  local copies, waits for them, and re-layouts: 14.3 us -> 32.9 us
  blocking collectives: 84.2 us -> 93.3 us
    ppermute x0 -> x7, waiting for transfers between devices: none -> 121 us  [ring_gather(): blocks.append(lax.ppermute(blocks[-1], axis, right))]
    all_gather x1, waiting for transfers between devices: 44 us -> 0.01 us  [per_device(): lax.all_gather(mlp_out, 'fsdp', axis=0, tiled=True)]
    all_gather x1, waiting for transfers between devices: 38.3 us -> 0.01 us  [per_device(): lax.all_gather(mlp_in, 'fsdp', axis=0, tiled=True)]
    all_gather x1, blocking collectives: 10.4 us -> 21.2 us  [per_device(): lax.all_gather(norm_attn, 'fsdp', axis=0, tiled=True)]
    unnamed x48 -> x67, local copies, waits for them, and re-layouts: 4.18 us -> 13.5 us
    all_gather x1, waiting for transfers between devices: 8.67 us -> 0.01 us  [per_device(): lax.all_gather(attn_in, 'fsdp', axis=0, tiled=True)]
  transfers between devices with their start and end apart: 9 -> 16, of which waited for: 6 -> 9; matrix products, arithmetic and copies ran while one was open for 26% -> 28% of each run, Pallas kernels for 0% -> 0%
where the time goes in v1:
time: 839 us; the launch traced here: 832 us
  waiting for transfers between devices  443 us (53%)
  matrix products  200 us (24%)
  blocking collectives  93.3 us (11%)
  other arithmetic  43.7 us (5%)
  local copies, waits for them, and re-layouts  32.9 us (4%)
  between operations  15.1 us (2%)
    ppermute x7, waiting for transfers between devices, ring_gather(): blocks.append(lax.ppermute(blocks[-1], axis, right))  121 us
    reduce_scatter x1, waiting for transfers between devices, per_device(): lax.psum_scatter(grad_up, 'fsdp', scatter_dimension=0, tiled=True)  117 us
    reduce_scatter x1, waiting for transfers between devices, per_device(): lax.psum_scatter(grad_down, 'fsdp', scatter_dimension=0, tiled=True)  102 us
    psum x1, waiting for transfers between devices, per_device(): lax.psum(shard_qkv.astype(jnp.bfloat16), 'dp').astype(jnp.float32)  100 us
    psum x1, blocking collectives, per_device(): grad_router = lax.psum(router_local, ('fsdp', 'dp'))  37.5 us
    all_gather x1, blocking collectives, per_device(): lax.all_gather(norm_attn, 'fsdp', axis=0, tiled=True)  21.2 us
    dot_general x1, matrix products, per_device(): jnp.einsum('kf,kd->fd', active, grad_expanded, preferred_element_type=jnp...  19.3 us
  transfers between devices with their start and end apart: 16, of which 9 were waited for; matrix products, arithmetic and copies ran while one was open for 28% of the time, Pallas kernels for 0%

profile of v1, /device:TPU:0, one launch (start us, length us, event | category | flops | bytes accessed | tf_op | source)
XLA Modules:
  0.0 832.1 jit_solution(5171738749583169594)
XLA Ops:
  10.1 18.8 %collective-permute-done = bf16[128,4096]{1,0:T(8,128)(2,1)S(1)} collective-permute-done((bf16[128,4096]{1,0:T(8,128)(2,1)}, bf16[128,4096]{1,0:T(8,128)(2,1)S(1)}, u32[]{:S(2)}, u32[]{:S(2)}) %collective-permute-start) | collective-permute-done | bytes 1048608 | tf_op jit(solution)/shard_map/ppermute | solution.py:23
  28.9 3.0 collective-permute-start.1
  31.9 7.1 multiply_reduce_fusion.7
  39.0 21.2 %all-gather = bf16[8,1,128]{2,1,0:T(2,128)(2,1)S(1)} all-gather(bf16[1,1,128]{2,1,0:T(2,128)(2,1)S(1)} %bitcast.104), channel_id=1, replica_groups=mesh['fsdp'=8,'dp'=4] {'fsdp'}, dimensions={0}, use_global_device_ids=true | all-gather | bytes 2304 | tf_op jit(solution)/shard_map/all_gather | solution.py:70
  60.2 9.6 %all-gather.1 = bf16[8,1,128]{2,1,0:T(2,128)(2,1)S(1)} all-gather(bf16[1,1,128]{2,1,0:T(2,128)(2,1)S(1)} %bitcast.105), channel_id=1, replica_groups=mesh['fsdp'=8,'dp'=4] {'fsdp'}, dimensions={0}, use_global_device_ids=true | all-gather | bytes 2304 | tf_op jit(solution)/shard_map/all_gather | solution.py:71
  71.2 9.2 %fusion.12 = f32[512,1024]{1,0:T(8,128)} fusion(bf16[4096,1024]{1,0:T(8,128)(2,1)} %param.12, s32[512]{0:T(512)S(1)} %copy-done.11), kind=kOutput, calls=%fused_computation.25 | convolution fusion | flops 4297064448 | bytes 10487808 | tf_op jit(solution)/shard_map/dot_general | solution.py:123
  80.4 8.6 %collective-permute-done.2 = bf16[128,4096]{1,0:T(8,128)(2,1)S(1)} collective-permute-done((bf16[128,4096]{1,0:T(8,128)(2,1)}, bf16[128,4096]{1,0:T(8,128)(2,1)S(1)}, u32[]{:S(2)}, u32[]{:S(2)}) %collective-permute-start.2) | collective-permute-done | bytes 1048608 | tf_op jit(solution)/shard_map/ppermute | solution.py:23
  90.1 19.4 %collective-permute-done.3 = bf16[128,4096]{1,0:T(8,128)(2,1)S(1)} collective-permute-done((bf16[128,4096]{1,0:T(8,128)(2,1)S(1)}, bf16[128,4096]{1,0:T(8,128)(2,1)S(1)}, u32[]{:S(2)}, u32[]{:S(2)}) %collective-permute-start.3) | collective-permute-done | bytes 1048608 | tf_op jit(solution)/shard_map/ppermute | solution.py:23
  110.5 2.4 bitcast_dynamic-update-slice_fusion.5
  112.9 23.0 %collective-permute-done.4 = bf16[128,4096]{1,0:T(8,128)(2,1)S(1)} collective-permute-done((bf16[128,4096]{1,0:T(8,128)(2,1)S(1)}, bf16[128,4096]{1,0:T(8,128)(2,1)S(1)}, u32[]{:S(2)}, u32[]{:S(2)}) %collective-permute-start.4) | collective-permute-done | bytes 1048608 | tf_op jit(solution)/shard_map/ppermute | solution.py:23
  138.0 34.5 %collective-permute-done.5 = bf16[128,4096]{1,0:T(8,128)(2,1)S(1)} collective-permute-done((bf16[128,4096]{1,0:T(8,128)(2,1)S(1)}, bf16[128,4096]{1,0:T(8,128)(2,1)S(1)}, u32[]{:S(2)}, u32[]{:S(2)}) %collective-permute-start.5) | collective-permute-done | bytes 1048608 | tf_op jit(solution)/shard_map/ppermute | solution.py:23
  175.0 16.9 %collective-permute-done.6 = bf16[128,4096]{1,0:T(8,128)(2,1)S(1)} collective-permute-done((bf16[128,4096]{1,0:T(8,128)(2,1)S(1)}, bf16[128,4096]{1,0:T(8,128)(2,1)S(1)}, u32[]{:S(2)}, u32[]{:S(2)}) %collective-permute-start.6) | collective-permute-done | bytes 1048608 | tf_op jit(solution)/shard_map/ppermute | solution.py:23
  192.9 8.2 gather_fusion
  201.1 6.6 convolution_convert_fusion
  211.0 2.3 copy.49
  215.5 8.5 %fusion.1 = (f32[16,512]{1,0:T(8,128)S(1)}, f32[16,512,512]{1,2,0:T(8,128)}) fusion(pred[512,512]{0,1:T(8,128)(4,1)S(1)} %compare_and_fusion, bf16[512,16,64]{0,2,1:T(8,128)(2,1)} %bitcast.76, bf16[512,16,64]{0,2,1:T(8,128)(2,1)S(1)} %bitcast.74), kind=kOutput, calls=%fused_computation.12 | convolution fusion | flops 549445632 | bytes 19169280 | tf_op jit(solution)/shard_map/qhd,khd->hqk/dot_general | solution.py:45
  224.0 9.2 %fusion = f32[16,512]{1,0:T(8,128)S(1)} fusion(f32[16,512,512]{1,2,0:T(8,128)} %get-tuple-element.31, f32[16,512]{1,0:T(8,128)S(1)} %get-tuple-element.30, pred[512,512]{0,1:T(8,128)(4,1)S(1)} %compare_and_fusion), kind=kLoop, calls=%fused_computation.9 | loop fusion | flops 16769024 | bytes 17104896 | tf_op jit(solution)/shard_map/reduce_sum | solution.py:94
  233.3 9.2 %fusion.23 = bf16[16,64,512]{2,1,0:T(8,128)(2,1)} fusion(bf16[512,16,64]{0,2,1:T(8,128)(2,1)} %bitcast.85, f32[16,512,512]{1,2,0:T(8,128)} %get-tuple-element.31, f32[16,512]{1,0:T(8,128)S(1)} %fusion, f32[16,512]{1,0:T(8,128)S(1)} %get-tuple-element.30, pred[512,512]{0,1:T(8,128)(4,1)S(1)} %compare_and_fusion), kind=kOutput, calls=%fused_computation.55 | convolution fusion | flops 558366720 | bytes 19202048 | tf_op jit(solution)/shard_map/hqk,khd->qhd/dot_general | solution.py:97
  242.5 4.5 multiply_reduce_fusion.6
  248.4 10.5 %fusion.52 = f32[512,4096]{1,0:T(8,128)} fusion(bf16[1024,4096]{1,0:T(8,128)(2,1)} %bitcast.78, f32[512,1024]{1,0:T(8,128)S(1)} %get-tuple-element.22, f32[1024]{0:T(1024)S(1)} %bitcast.94, f32[512]{0:T(512)S(1)} %fusion.39), kind=kOutput, calls=%fused_computation.104 | convolution fusion | flops 4296540160 | bytes 18880512 | tf_op jit(solution)/shard_map/dot_general | solution.py:105
  258.8 14.4 %fusion.8 = bf16[512,4096]{1,0:T(8,128)(2,1)} fusion(f32[512,4096]{1,0:T(8,128)} %fusion.52, bf16[4096,1024]{1,0:T(8,128)(2,1)} %all-gather.11.cloned.1.call-done, f32[512,1024]{1,0:T(8,128)} %fusion.12, f32[512]{0:T(512)S(1)} %bitcast.99), kind=kOutput, calls=%fused_computation.19 | convolution fusion | flops 4337958912 | bytes 23070720 | tf_op jit(solution)/shard_map/kd,fd->kf/dot_general | solution.py:128
  273.2 10.1 %multiply_reduce_fusion.1 = (f32[1024]{0:T(1024)S(1)}, f32[512]{0:T(512)S(1)}, f32[512,1024]{1,0:T(8,128)S(1)}) fusion(f32[512,1024]{1,0:T(8,128)} %copy-done.1, f32[512]{0:T(512)S(1)} %fusion.39, f32[1024]{0:T(1024)S(1)} %bitcast.95, bf16[512,4096]{1,0:T(8,128)(2,1)} %fusion.8, bf16[1024,4096]{1,0:T(8,128)(2,1)} %all-gather.13.cloned.1.call-done), kind=kOutput, calls=%fused_computation.40 | convolution fusion | flops 4298111488 | bytes 16789504 | tf_op jit(solution)/shard_map/kf,df->kd/dot_general | solution.py:134
  283.4 10.4 %multiply_reduce_fusion.3 = (f32[512]{0:T(512)S(1)}, bf16[512,1024]{1,0:T(8,128)(2,1)S(1)}, f32[512,1024]{1,0:T(8,128)}) fusion(f32[512,1024]{1,0:T(8,128)S(1)} %copy-done.24, f32[512,1024]{1,0:T(8,128)S(1)} %copy-done.2, f32[512]{0:T(512)S(1)} %multiply_multiply_fusion.3, f32[512]{0:T(512)S(1)} %fusion.39, f32[512,1024]{1,0:T(8,128)S(1)} %get-tuple-element.33, ...), kind=kOutput, calls=%fused_computation.42 | convolution fusion | flops 4319608320 | bytes 28323840 | tf_op jit(solution)/shard_map/dot_general | solution.py:108
  294.8 3.2 fusion.54
  298.1 4.2 convolution_convert_fusion.1
  302.2 2.3 copy.52
  304.6 13.4 %multiply_reduce_fusion = (f32[16,512]{1,0:T(8,128)S(1)}, f32[16,512,512]{1,2,0:T(8,128)}) fusion(f32[16,512]{1,0:T(8,128)S(1)} %log_add_fusion, f32[16,512,512]{1,2,0:T(8,128)} %get-tuple-element.31, pred[512,512]{0,1:T(8,128)(4,1)S(1)} %compare_and_fusion, bf16[512,16,64]{0,2,1:T(8,128)(2,1)} %bitcast.87, bf16[512,16,64]{0,2,1:T(8,128)(2,1)} %bitcast.86), kind=kOutput, calls=%fused_computation.3 | convolution fusion | flops 562028544 | bytes 35979264 | tf_op jit(solution)/shard_map/qhd,khd->hqk/dot_general | solution.py:146
  318.0 13.1 %multiply_convert_fusion = bf16[16,512,512]{1,2,0:T(8,128)(2,1)S(1)} fusion(f32[16,512,512]{1,2,0:T(8,128)} %get-tuple-element.36, f32[16,512]{1,0:T(8,128)S(1)} %get-tuple-element.35, f32[16,512]{1,0:T(8,128)S(1)} %log_add_fusion, f32[16,512,512]{1,2,0:T(8,128)} %get-tuple-element.31, pred[512,512]{0,1:T(8,128)(4,1)S(1)} %compare_and_fusion), kind=kLoop, calls=%fused_computation.2 | loop fusion | flops 29360128 | bytes 42270720 | tf_op jit(solution)/shard_map/convert_element_type | solution.py:150
  331.1 2.6 multiply_convert_fusion.2
  335.3 8.7 %fusion.24 = bf16[16,64,512]{2,1,0:T(8,128)(2,1)S(1)} fusion(bf16[512,16,64]{0,2,1:T(8,128)(2,1)S(1)} %bitcast.88, f32[16,512]{1,0:T(8,128)S(1)} %log_add_fusion, f32[16,512,512]{1,2,0:T(8,128)} %get-tuple-element.31, pred[512,512]{0,1:T(8,128)(4,1)S(1)} %compare_and_fusion), kind=kOutput, calls=%fused_computation.57 | convolution fusion | flops 558366720 | bytes 19169280 | tf_op jit(solution)/shard_map/hqk,qhd->khd/dot_general | solution.py:160
  345.0 9.9 %fusion.27 = f32[1024,3072]{1,0:T(8,128)} fusion(bf16[512,1024]{0,1:T(8,128)(2,1)S(1)} %bitcast.108, bf16[512,1024]{0,1:T(8,128)(2,1)S(1)} %bitcast.83, bf16[512,1024]{0,1:T(8,128)(2,1)S(1)} %bitcast.79, f32[512,1024]{1,0:T(8,128)S(1)} %get-tuple-element.29, f32[1024]{0:T(1024)S(1)} %bitcast.91, f32[512]{0:T(512)S(1)} %fusion.38), kind=kOutput, calls=%fused_computation.58 | convolution fusion | flops 3232235520 | bytes 17831936 | tf_op jit(solution)/shard_map/kd,ke->de/dot_general | solution.py:171
  355.0 19.3 %fusion.49 = f32[4096,1024]{1,0:T(8,128)} fusion(f32[512,1024]{1,0:T(8,128)} %fusion.12, f32[512]{0:T(512)S(1)} %bitcast.101, f32[512,4096]{1,0:T(8,128)} %fusion.52), kind=kOutput, calls=%fused_computation.101 | convolution fusion | flops 4314890240 | bytes 27265024 | tf_op jit(solution)/shard_map/kf,kd->fd/dot_general | solution.py:127
  374.6 15.0 %fusion.51 = f32[1024,4096]{1,0:T(8,128)} fusion(bf16[512,4096]{1,0:T(8,128)(2,1)} %fusion.8, f32[512,1024]{1,0:T(8,128)} %copy-done.1, f32[1024]{0:T(1024)S(1)} %bitcast.97, f32[512]{0:T(512)S(1)} %fusion.39), kind=kOutput, calls=%fused_computation.103 | convolution fusion | flops 4296540160 | bytes 23074816 | tf_op jit(solution)/shard_map/kd,kf->df/dot_general | solution.py:133
  391.5 8.4 %multiply_reduce_fusion.2 = (f32[1024]{0:T(1024)S(1)}, f32[512]{0:T(512)S(1)}, f32[512,1024]{1,0:T(8,128)}) fusion(f32[512,1024]{1,0:T(8,128)S(1)} %get-tuple-element.29, f32[512]{0:T(512)S(1)} %fusion.38, f32[1024]{0:T(1024)S(1)} %bitcast.92, bf16[1024,3072]{1,0:T(8,128)(2,1)} %all-gather.7.cloned.1.call-done, bf16[512,1024]{0,1:T(8,128)(2,1)} %bitcast.109, ...), kind=kOutput, calls=%fused_computation.41 | convolution fusion | flops 3233806848 | bytes 13643776 | tf_op jit(solution)/shard_map/ke,de->kd/dot_general | solution.py:172
  400.0 13.3 %all-reduce.2 = (bf16[1024]{0:T(1024)(128)(2,1)S(1)}, bf16[1024]{0:T(1024)(128)(2,1)S(1)}) all-reduce(f32[1024]{0:T(1024)S(1)} %get-tuple-element.11, f32[1024]{0:T(1024)S(1)} %get-tuple-element.9), channel_id=6, replica_groups=mesh['fsdp'=8,'dp'=4] {'fsdp'}, use_global_device_ids=true, to_apply=%region_19.20.clone | all-reduce | flops 2048 | bytes 12288
  413.4 11.7 %all-reduce.3 = (bf16[128]{0:T(256)(128)(2,1)S(1)}, bf16[128]{0:T(256)(128)(2,1)S(1)}) all-reduce(bf16[128]{0:T(256)(128)(2,1)S(1)} %dynamic-slice.7, bf16[128]{0:T(256)(128)(2,1)S(1)} %dynamic-slice.6), channel_id=1, replica_groups=mesh['fsdp'=8,'dp'=4] {'dp'}, use_global_device_ids=true, to_apply=%region_20.21 | all-reduce | flops 256 | bytes 1024 | tf_op jit(solution)/shard_map/psum | solution.py:197
  427.2 37.5 %psum.55 = f32[1024]{0:T(1024)} all-reduce(f32[1024]{0:T(1024)S(1)} %bitcast.89), channel_id=1, replica_groups=mesh['fsdp'=8,'dp'=4] {'fsdp','dp'}, use_global_device_ids=true, to_apply=%region_24.25 | all-reduce | flops 1024 | bytes 8192 | tf_op jit(solution)/shard_map/psum | solution.py:200
  466.7 2.7 convert_element_type.138
  469.4 102.1 %reduce-scatter.11.cloned.1.call-done = f32[512,1024]{1,0:T(8,128)} async-done(((f32[4096,1024]{1,0:T(8,128)}), f32[512,1024]{1,0:T(8,128)}) %reduce-scatter.11.cloned.1.call-update) | async-done | bytes 2097168 | tf_op jit(solution)/shard_map/reduce_scatter | solution.py:184
  571.5 2.7 convert_element_type.144
  574.3 117.0 %reduce-scatter.9.cloned.1.call-done = f32[128,4096]{1,0:T(8,128)} async-done(((f32[1024,4096]{1,0:T(8,128)}), f32[128,4096]{1,0:T(8,128)}) %reduce-scatter.9.cloned.1.call-update) | async-done | bytes 2097168 | tf_op jit(solution)/shard_map/reduce_scatter | solution.py:183
  691.3 2.7 convert_element_type.142
  694.0 10.0 %add_convert_fusion.1 = bf16[4096,1024]{1,0:T(8,128)(2,1)} fusion(bf16[4096,1024]{1,0:T(8,128)(2,1)} %param.11, s32[512]{0:T(512)S(1)} %copy-done.12, f32[512,1024]{1,0:T(8,128)} %get-tuple-element.34, f32[512]{0:T(512)S(1)} %bitcast.102), kind=kOutput, calls=%fused_computation.5 | convolution fusion | flops 4310695936 | bytes 18878464 | tf_op jit(solution)/shard_map/kt,kd->td/dot_general | solution.py:113
  704.1 11.4 %add_convert_fusion = bf16[4096,1024]{1,0:T(8,128)(2,1)} fusion(bf16[4096,1024]{1,0:T(8,128)(2,1)} %param.12, s32[512]{0:T(512)S(1)} %copy-done.12, f32[512,1024]{1,0:T(8,128)S(1)} %get-tuple-element.29, f32[512,1024]{1,0:T(8,128)S(1)} %copy-done.25, f32[1024]{0:T(1024)S(1)} %convert_element_type.135, f32[512]{0:T(512)S(1)} %get-tuple-element.26, ...), kind=kOutput, calls=%fused_computation.1 | convolution fusion | flops 4316987392 | bytes 25190400 | tf_op jit(solution)/shard_map/kt,kd->td/dot_general | solution.py:179
  715.5 100.1 %all-reduce.7.cloned.1.call-done = (bf16[128,3072]{1,0:T(8,128)(2,1)}, bf16[128,1024]{1,0:T(8,128)(2,1)}, bf16[128,4096]{1,0:T(8,128)(2,1)}, bf16[512,1024]{1,0:T(8,128)(2,1)}) async-done(((bf16[128,3072]{1,0:T(8,128)(2,1)}, bf16[128,1024]{1,0:T(8,128)(2,1)}, bf16[128,4096]{1,0:T(8,128)(2,1)}, bf16[512,1024]{1,0:T(8,128)(2,1)}), (bf16[128,3072]{1,0:T(8,128)(2,1)}, bf16[128,1024]{1,0:T(8,128)(2,1)}, ...) | async-done | bytes 3145744 | tf_op jit(solution)/shard_map/psum | solution.py:193
  817.4 2.4 convert_element_type.139
  819.8 2.8 convert_element_type.143
  822.6 2.8 convert_element_type.145
  (121 shorter events, 30.1 us)
Async XLA Ops:
  7.2 193.9 %all-gather.7.cloned.1.call-start = ((), (), s32[]{:S(2)}) async-start(), calls=%async_computation.4 | async-start | bytes 7077888 | tf_op jit(solution)/shard_map/all_gather | solution.py:68
  7.9 234.6 %all-gather.9.cloned.1.call-start = ((), (), s32[]{:S(2)}) async-start(), calls=%async_computation.5 | async-start | bytes 2359296 | tf_op jit(solution)/shard_map/all_gather | solution.py:69
  8.7 250.2 %all-gather.11.cloned.1.call-start = ((), (), s32[]{:S(2)}) async-start(), calls=%async_computation.6 | async-start | bytes 9437184 | tf_op jit(solution)/shard_map/all_gather | solution.py:75
  9.4 263.8 %all-gather.13.cloned.1.call-start = ((), (), s32[]{:S(2)}) async-start(), calls=%async_computation.7 | async-start | bytes 9437184 | tf_op jit(solution)/shard_map/all_gather | solution.py:120
  9.4 19.5 %collective-permute-start = (bf16[128,4096]{1,0:T(8,128)(2,1)}, bf16[128,4096]{1,0:T(8,128)(2,1)S(1)}, u32[]{:S(2)}, u32[]{:S(2)}) collective-permute-start(bf16[128,4096]{1,0:T(8,128)(2,1)} %param.17), channel_id=1, source_target_pairs={{0,4},{4,8},{8,12},{12,16},{16,20},{20,24},{24,28},{28,0},{1,5},{5... | collective-permute-start | bytes 3145736 | tf_op jit(solution)/shard_map/ppermute | solution.py:23
  10.0 29.0 %copy-start.17 = (bf16[128]{0:T(256)(128)(2,1)S(1)}, bf16[128]{0:T(256)(128)(2,1)}, u32[]{:S(2)}) copy-start(bf16[128]{0:T(256)(128)(2,1)} %param.19) | copy-start | bytes 772
  10.0 50.2 %copy-start.18 = (bf16[128]{0:T(256)(128)(2,1)S(1)}, bf16[128]{0:T(256)(128)(2,1)}, u32[]{:S(2)}) copy-start(bf16[128]{0:T(256)(128)(2,1)} %param.20) | copy-start | bytes 772
  10.0 59.8 %copy-start.13 = (bf16[1024]{0:T(1024)(128)(2,1)S(1)}, bf16[1024]{0:T(1024)(128)(2,1)}, u32[]{:S(2)}) copy-start(bf16[1024]{0:T(1024)(128)(2,1)} %param.21) | copy-start | bytes 6148
  10.0 59.8 %copy-start.20 = (s32[8]{0:T(128)S(1)}, s32[8]{0:T(128)}, u32[]{:S(2)}) copy-start(s32[8]{0:T(128)} %param.13) | copy-start | bytes 100
  10.1 60.0 %copy-start.11 = (s32[512]{0:T(512)S(1)}, s32[512]{0:T(512)}, u32[]{:S(2)}) copy-start(s32[512]{0:T(512)} %param.14) | copy-start | bytes 6148
  10.1 454.7 %reduce-scatter.7.cloned.1.call-start = ((), (), s32[]{:S(2)}) async-start(), calls=%async_computation.9 | async-start | bytes 4718592 | tf_op jit(solution)/shard_map/reduce_scatter | solution.py:189
  28.9 41.9 %collective-permute-start.1 = (bf16[128,4096]{1,0:T(8,128)(2,1)S(1)}, bf16[128,4096]{1,0:T(8,128)(2,1)}, u32[]{:S(2)}, u32[]{:S(2)}) collective-permute-start(bf16[128,4096]{1,0:T(8,128)(2,1)S(1)} %collective-permute-done), channel_id=1, source_target_pairs={{0,4},{4,8},{8,12},{12,16},{16,20},{20,24},{24,28},{28,0},{1,5},{5... | collective-permute-start | bytes 3145736 | tf_op jit(solution)/shard_map/ppermute | solution.py:23
  39.0 31.1 %copy-start.15 = (f32[512]{0:T(512)}, f32[512]{0:T(512)S(1)}, u32[]{:S(2)}) copy-start(f32[512]{0:T(512)S(1)} %get-tuple-element.28) | copy-start | bytes 6148
  70.8 18.2 %copy-start.5 = (bf16[128,4096]{1,0:T(8,128)(2,1)S(1)}, bf16[128,4096]{1,0:T(8,128)(2,1)}, u32[]{:S(2)}) copy-start(bf16[128,4096]{1,0:T(8,128)(2,1)} %param.17) | copy-start | bytes 3145732
  70.8 18.2 %collective-permute-start.2 = (bf16[128,4096]{1,0:T(8,128)(2,1)}, bf16[128,4096]{1,0:T(8,128)(2,1)S(1)}, u32[]{:S(2)}, u32[]{:S(2)}) collective-permute-start(bf16[128,4096]{1,0:T(8,128)(2,1)} %collective-permute-done.1), channel_id=1, source_target_pairs={{0,4},{4,8},{8,12},{12,16},{16,20},{20,24},{24,28},{28,0},{1,5},{5... | collective-permute-start | bytes 3145736 | tf_op jit(solution)/shard_map/ppermute | solution.py:23
  89.0 20.5 %collective-permute-start.3 = (bf16[128,4096]{1,0:T(8,128)(2,1)S(1)}, bf16[128,4096]{1,0:T(8,128)(2,1)S(1)}, u32[]{:S(2)}, u32[]{:S(2)}) collective-permute-start(bf16[128,4096]{1,0:T(8,128)(2,1)S(1)} %collective-permute-done.2), channel_id=1, source_target_pairs={{0,4},{4,8},{8,12},{12,16},{16,20},{20,24},{24,28},{28,0},{1,5},{5... | collective-permute-start | bytes 3145736 | tf_op jit(solution)/shard_map/ppermute | solution.py:23
  109.5 26.4 %collective-permute-start.4 = (bf16[128,4096]{1,0:T(8,128)(2,1)S(1)}, bf16[128,4096]{1,0:T(8,128)(2,1)S(1)}, u32[]{:S(2)}, u32[]{:S(2)}) collective-permute-start(bf16[128,4096]{1,0:T(8,128)(2,1)S(1)} %collective-permute-done.3), channel_id=1, source_target_pairs={{0,4},{4,8},{8,12},{12,16},{16,20},{20,24},{24,28},{28,0},{1,5},{5... | collective-permute-start | bytes 3145736 | tf_op jit(solution)/shard_map/ppermute | solution.py:23
  135.8 36.6 %collective-permute-start.5 = (bf16[128,4096]{1,0:T(8,128)(2,1)S(1)}, bf16[128,4096]{1,0:T(8,128)(2,1)S(1)}, u32[]{:S(2)}, u32[]{:S(2)}) collective-permute-start(bf16[128,4096]{1,0:T(8,128)(2,1)S(1)} %collective-permute-done.4), channel_id=1, source_target_pairs={{0,4},{4,8},{8,12},{12,16},{16,20},{20,24},{24,28},{28,0},{1,5},{5... | collective-permute-start | bytes 3145736 | tf_op jit(solution)/shard_map/ppermute | solution.py:23
  172.4 19.4 %collective-permute-start.6 = (bf16[128,4096]{1,0:T(8,128)(2,1)S(1)}, bf16[128,4096]{1,0:T(8,128)(2,1)S(1)}, u32[]{:S(2)}, u32[]{:S(2)}) collective-permute-start(bf16[128,4096]{1,0:T(8,128)(2,1)S(1)} %collective-permute-done.5), channel_id=1, source_target_pairs={{0,4},{4,8},{8,12},{12,16},{16,20},{20,24},{24,28},{28,0},{1,5},{5... | collective-permute-start | bytes 3145736 | tf_op jit(solution)/shard_map/ppermute | solution.py:23
  247.0 1.3 copy-start.1
  273.2 10.2 %copy-start.2 = (f32[512,1024]{1,0:T(8,128)S(1)}, f32[512,1024]{1,0:T(8,128)}, u32[]{:S(2)}) copy-start(f32[512,1024]{1,0:T(8,128)} %copy-done.1) | copy-start | bytes 6291460
  273.2 10.2 %copy-start.4 = (f32[512,1024]{1,0:T(8,128)S(1)}, f32[512,1024]{1,0:T(8,128)}, u32[]{:S(2)}) copy-start(f32[512,1024]{1,0:T(8,128)} %get-tuple-element.32) | copy-start | bytes 6291460
  273.2 10.2 %copy-start.19 = (bf16[4096,1024]{1,0:T(8,128)(2,1)S(1)}, bf16[4096,1024]{1,0:T(8,128)(2,1)}, u32[]{:S(2)}) copy-start(bf16[4096,1024]{1,0:T(8,128)(2,1)} %all-gather.11.cloned.1.call-done) | copy-start | bytes 25165828
  273.2 10.2 %copy-start.24 = (f32[512,1024]{1,0:T(8,128)S(1)}, f32[512,1024]{1,0:T(8,128)}, u32[]{:S(2)}) copy-start(f32[512,1024]{1,0:T(8,128)} %fusion.12) | copy-start | bytes 6291460
  283.4 10.4 %copy-start.26 = (f32[512,1024]{1,0:T(8,128)}, f32[512,1024]{1,0:T(8,128)S(1)}, u32[]{:S(2)}) copy-start(f32[512,1024]{1,0:T(8,128)S(1)} %get-tuple-element.33) | copy-start | bytes 6291460
  283.4 11.4 %copy-start.8 = (bf16[16,64,512]{2,1,0:T(8,128)(2,1)S(1)}, bf16[16,64,512]{2,1,0:T(8,128)(2,1)}, u32[]{:S(2)}) copy-start(bf16[16,64,512]{2,1,0:T(8,128)(2,1)} %fusion.23) | copy-start | bytes 3145732
  293.8 1.0 copy-start.23
  304.6 162.1 %reduce-scatter.5.cloned.1.call-start = ((), (), s32[]{:S(2)}) async-start(), calls=%async_computation.8 | async-start | bytes 14155776 | tf_op jit(solution)/shard_map/reduce_scatter | solution.py:188
  318.0 13.1 %copy-start = (bf16[512,1024]{0,1:T(8,128)(2,1)S(1)}, bf16[512,1024]{0,1:T(8,128)(2,1)}, u32[]{:S(2)}) copy-start(bf16[512,1024]{0,1:T(8,128)(2,1)} %copy.49) | copy-start | bytes 3145732
  333.7 10.3 %copy-start.9 = (bf16[16,64,512]{2,1,0:T(8,128)(2,1)}, bf16[16,64,512]{2,1,0:T(8,128)(2,1)S(1)}, u32[]{:S(2)}) copy-start(bf16[16,64,512]{2,1,0:T(8,128)(2,1)S(1)} %multiply_convert_fusion.2) | copy-start | bytes 3145732
  333.7 1.6 copy-start.10
  335.3 8.7 %copy-start.6 = (bf16[16,64,512]{2,1,0:T(8,128)(2,1)}, bf16[16,64,512]{2,1,0:T(8,128)(2,1)S(1)}, u32[]{:S(2)}) copy-start(bf16[16,64,512]{2,1,0:T(8,128)(2,1)S(1)} %multiply_convert_fusion.3) | copy-start | bytes 3145732
  344.0 1.0 copy-start.21
  354.9 216.6 %reduce-scatter.11.cloned.1.call-start = ((), (), s32[]{:S(2)}) async-start(), calls=%async_computation.11 | async-start | bytes 18874368 | tf_op jit(solution)/shard_map/reduce_scatter | solution.py:184
  374.3 317.0 %reduce-scatter.9.cloned.1.call-start = ((), (), s32[]{:S(2)}) async-start(), calls=%async_computation.10 | async-start | bytes 18874368 | tf_op jit(solution)/shard_map/reduce_scatter | solution.py:183
  389.6 0.7 copy-start.14
  389.6 0.7 copy-start.22
  389.6 1.9 copy-start.7
  389.6 426.0 %all-reduce.7.cloned.1.call-start = ((), (), s32[]{:S(2)}) async-start(), calls=%async_computation.12 | async-start | bytes 6291456 | tf_op jit(solution)/shard_map/psum | solution.py:193
  391.5 73.3 %copy-start.16 = (f32[512]{0:T(512)S(1)}, f32[512]{0:T(512)}, u32[]{:S(2)}) copy-start(f32[512]{0:T(512)} %copy-done.15) | copy-start | bytes 6148
  400.0 294.0 %copy-start.12 = (s32[512]{0:T(512)S(1)}, s32[512]{0:T(512)}, u32[]{:S(2)}) copy-start(s32[512]{0:T(512)} %param.14) | copy-start | bytes 6148
  694.0 10.1 %copy-start.3 = (f32[512,1024]{1,0:T(8,128)S(1)}, f32[512,1024]{1,0:T(8,128)}, u32[]{:S(2)}) copy-start(f32[512,1024]{1,0:T(8,128)} %copy-done.1) | copy-start | bytes 6291460
  694.0 10.1 %copy-start.25 = (f32[512,1024]{1,0:T(8,128)S(1)}, f32[512,1024]{1,0:T(8,128)}, u32[]{:S(2)}) copy-start(f32[512,1024]{1,0:T(8,128)} %get-tuple-element.37) | copy-start | bytes 6291460
  694.0 10.0 %copy-start.27 = (f32[512,1024]{1,0:T(8,128)S(1)}, f32[512,1024]{1,0:T(8,128)}, u32[]{:S(2)}) copy-start(f32[512,1024]{1,0:T(8,128)} %copy-done.26) | copy-start | bytes 6291460
Sparse Core Ops, SparseCore 0:
  9.9 56.8 all-gather.6
  68.6 33.1 all-gather.8
  103.7 69.3 all-gather.10
  174.8 55.5 all-gather.12
  304.7 50.3 reduce-scatter.6
  358.5 93.2 reduce-scatter.4
  455.4 116.1 reduce-scatter.10
  575.1 116.1 reduce-scatter.8
  694.5 121.0 all-reduce.6
